TPU v7x, 128 devices: a whole 4x4x4 slice. The times are simulated.
128 devices in a mesh: tm: 32 (over x, z, core), feat: 4 (over y).
Axes of the slice: x: 4, y: 4, z: 4, core: 2. Of those that a mesh axis runs over, the one named last changes fastest.
Arguments:
- activations: bfloat16 [81920, 2048], P(('tm', 'feat')), may hold values from -19 to 19
- targets: bfloat16 [81920, 128], P(('tm', 'feat')), may hold values from -8 to 8
- span_of: int32 [81920], P(('tm', 'feat')), may hold values from 0 to 31, as said below
Outputs:
- predictions: bfloat16 [81920, 128], P(('tm', 'feat'))
- surprise: float32 [81920], P(('tm', 'feat'))
Inputs may be any that keep to these rules, and one draw needn't show every extreme that they name: `span_of`: in each aligned block of 640 rows (the rows of one device) every span from 0 to 31 appears exactly 20 times.
All inputs are finite; a program needn't handle non-finite values.
Results may differ from a plain program's by a relative error of at most 0.0049.
Values may be sent and summed in bfloat16 or wider, within the bound.
No kernel may reach another device: no remote copies, remote signals or barrier semaphores. Data moves between devices by JAX's collectives and lax.ppermute only.
A program may use at most 320 MiB of HBM per device.

v0:
```python
import jax
import jax.numpy as jnp
from jax import lax
from jax.sharding import Mesh, PartitionSpec as P

ITERS = 3
RIDGE = 0.1
TINY = 1e-06
TM = ("x", "z", "c")
SWAP = [(0, 1), (1, 0)]


def masked_sum(stack, position):
    keep = jnp.arange(stack.shape[0]) < position
    return jnp.sum(jnp.where(keep.reshape((-1,) + (1,) * (stack.ndim - 1)), stack, 0.0), axis=0)


def gather_feat(piece):
    n = lax.axis_size("feat")
    parts = [piece] + [
        lax.ppermute(piece, "feat", [(i, (i - k) % n) for i in range(n)]) for k in range(1, n)
    ]
    return jnp.concatenate(parts, axis=0)


def rotate(a, start, size, axis):
    return lax.dynamic_slice_in_dim(jnp.concatenate([a, a], axis=axis), start, size, axis)


def exclusive_prefix(block):
    ci = lax.axis_index("c")
    zi = lax.axis_index("z")
    xi = lax.axis_index("x")
    rows = block.shape[0]
    half = rows // 2
    partner = lax.ppermute(block, "c", SWAP)
    chip = block + partner
    below = jnp.where(ci == 1, partner, 0.0)
    mine = lax.dynamic_slice_in_dim(chip, ci * half, half, 0)
    along_z = lax.all_gather(mine, "z")
    before_z = masked_sum(along_z, zi)
    total_z = jnp.sum(along_z, axis=0)
    quarter = half // lax.axis_size("z")
    piece = lax.dynamic_slice_in_dim(total_z, zi * quarter, quarter, 0)
    along_x = lax.all_gather(piece, "x")
    before_x = lax.all_gather(masked_sum(along_x, xi), "z", axis=0, tiled=True)
    mine_prefix = before_x + before_z
    other_prefix = lax.ppermute(mine_prefix, "c", SWAP)
    first = ci == 0
    top = jnp.where(first, mine_prefix, other_prefix)
    bottom = jnp.where(first, other_prefix, mine_prefix)
    return jnp.concatenate([top, bottom], axis=0) + below


def body(activations, targets, span_of):
    spans = lax.axis_size(TM)
    feat_count = lax.axis_size("feat")
    tok_dev, width = activations.shape
    n_targets = targets.shape[1]
    block_rows = width // feat_count
    share = tok_dev // spans
    contract = (((0,), (0,)), ((), ()))
    highest = lax.Precision.HIGHEST
    hot = (span_of[:, None] == jnp.arange(spans)[None, :]).astype(jnp.float32)
    earlier = (jnp.arange(tok_dev)[:, None] > jnp.arange(tok_dev)[None, :]).astype(jnp.float32)
    before = jnp.dot(earlier, hot, precision=highest, preferred_element_type=jnp.float32)
    rank = jnp.sum(before * hot, axis=1).astype(jnp.int32)
    dest = span_of * share + rank
    permute = (dest[None, :] == jnp.arange(tok_dev)[:, None]).astype(jnp.bfloat16)
    joined_in = jnp.concatenate([activations, targets], axis=1)
    sorted_xy = jnp.dot(permute, joined_in, preferred_element_type=jnp.float32).astype(jnp.bfloat16)
    sorted_xy = sorted_xy.reshape(spans, share, width + n_targets)
    moved = lax.all_to_all(sorted_xy, TM, split_axis=0, concat_axis=0, tiled=True)
    local_xy = moved.reshape(tok_dev, width + n_targets)
    local_x = local_xy[:, :width]
    col_start = lax.axis_index("feat") * block_rows
    rows_xy = lax.all_gather(local_xy, "feat", axis=0, tiled=True)
    own = lax.dynamic_slice_in_dim(rows_xy, col_start, block_rows, 1)
    moments = exclusive_prefix(
        lax.dot_general(own, rows_xy, contract, preferred_element_type=jnp.float32)
    )
    fi = lax.axis_index("feat")
    gram_prefix = rotate(moments[:, :width], fi * block_rows, width, 1)
    cross_prefix = gather_feat(moments[:, width:])
    span = (lax.axis_index("x") * lax.axis_size("z") + lax.axis_index("z")) * lax.axis_size(
        "c"
    ) + lax.axis_index("c")
    seen = (span * (tok_dev * feat_count)).astype(jnp.float32)
    scale = 1.0 / jnp.maximum(seen, 1.0)
    rhs = scale * cross_prefix
    residual = rhs
    direction = rhs
    norm_now = jnp.sum(residual * residual, axis=0)
    solution = None
    for step in range(ITERS):
        product = jnp.dot(
            gram_prefix, direction, precision=lax.Precision.HIGH, preferred_element_type=jnp.float32
        )
        own_image = scale * product + RIDGE * direction[:block_rows]
        if step + 1 < ITERS:
            image = gather_feat(own_image)
            curvature = jnp.sum(direction * image, axis=0)
        else:
            partial = jnp.sum(direction[:block_rows] * own_image, axis=0, keepdims=True)
            curvature = jnp.sum(gather_feat(partial), axis=0)
        alpha = norm_now / (curvature + TINY)
        update = alpha * direction
        solution = update if solution is None else solution + update
        if step + 1 < ITERS:
            residual = residual - alpha * image
            norm_next = jnp.sum(residual * residual, axis=0)
            direction = residual + norm_next / (norm_now + TINY) * direction
            norm_now = norm_next
    weights = rotate(
        solution.astype(jnp.bfloat16), (feat_count - fi) % feat_count * block_rows, width, 0
    )
    predicted = jnp.dot(local_x, weights, preferred_element_type=jnp.float32).astype(jnp.bfloat16)
    returned = lax.all_to_all(
        predicted.reshape(spans, share, n_targets), TM, split_axis=0, concat_axis=0, tiled=True
    )
    in_order = returned.reshape(tok_dev, n_targets)
    predictions = lax.dot_general(
        permute, in_order, (((0,), (0,)), ((), ())), preferred_element_type=jnp.float32
    ).astype(jnp.bfloat16)
    error = targets.astype(jnp.float32) - predictions.astype(jnp.float32)
    surprise = jnp.mean(error * error, axis=1)
    return (predictions, surprise)


def solution(mesh):
    tm = mesh.shape["tm"]
    feat = mesh.shape["feat"]
    fine = Mesh(mesh.devices.reshape(tm // 8, 4, 2, feat), TM + ("feat",))
    rows = TM + ("feat",)
    return jax.shard_map(
        body,
        mesh=fine,
        in_specs=(P(rows, None), P(rows, None), P(rows)),
        out_specs=(P(rows, None), P(rows)),
        check_vma=False,
    )
```

profile of v0, /device:TPU:1, one launch (start us, length us, event | category | flops | bytes accessed | tf_op | source)
XLA Modules:
  0.0 470.7 jit_solution(7356976778085991904)
XLA Ops:
  7.2 1.1 fusion.20
  8.3 0.7 convert_add_fusion
  9.0 5.8 %convolution_convert_fusion = bf16[640,2176]{1,0:T(8,128)(2,1)} fusion(bf16[640,128]{1,0:T(8,128)(2,1)} %param.4, bf16[640,2048]{1,0:T(8,128)(2,1)} %param.3, s32[640]{0:T(1024)S(1)} %convert_add_fusion), kind=kOutput, calls=%fused_computation.3 | convolution fusion | flops 1789952000 | bytes 5573120 | tf_op jit(solution)/shard_map/dot_general | solution.py:71
  14.8 3.6 reshape.65
  18.3 51.3 %all_to_all.10 = bf16[32,20,2176]{2,1,0:T(8,128)(2,1)} all-to-all(bf16[32,20,2176]{2,1,0:T(8,128)(2,1)S(1)} %reshape.65), channel_id=1, replica_groups=mesh['x'=4,'z'=4,'c'=2,'feat'=4] {'x','z','c'}, dimensions={0} | all-to-all | bytes 5570560 | tf_op jit(solution)/shard_map/all_to_all | solution.py:73
  69.7 5.3 %reshape.66 = bf16[640,2176]{1,0:T(8,128)(2,1)} reshape(bf16[32,20,2176]{2,1,0:T(8,128)(2,1)} %all_to_all.10) | data formatting | bytes 5570560 | tf_op jit(solution)/shard_map/reshape | solution.py:74
  75.0 103.8 %all-gather.7.cloned.1.call-done = bf16[2560,2176]{1,0:T(8,128)(2,1)} async-done(((bf16[640,2176]{1,0:T(8,128)(2,1)}), bf16[2560,2176]{1,0:T(8,128)(2,1)}) %all-gather.7.cloned.1.call-update) | async-done | bytes 11141136 | tf_op jit(solution)/shard_map/all_gather | solution.py:77
  178.8 12.5 %fusion.6 = f32[512,2176]{1,0:T(8,128)} fusion(bf16[2560,2176]{1,0:T(8,128)(2,1)} %all-gather.7.cloned.1.call-done, s32[]{:T(128)S(6)} %select_n.51), kind=kOutput, calls=%fused_computation.11 | convolution fusion | flops 5704253440 | bytes 18219012 | tf_op jit(solution)/shard_map/dot_general | solution.py:80
  191.2 0.8 collective-permute-start
  192.1 7.5 %collective-permute-done = f32[512,2176]{1,0:T(8,128)} collective-permute-done((f32[512,2176]{1,0:T(8,128)}, f32[512,2176]{1,0:T(8,128)}, u32[]{:S(2)}, u32[]{:S(2)}) %collective-permute-start) | collective-permute-done | bytes 4456480 | tf_op jit(solution)/shard_map/ppermute | solution.py:36
  199.6 3.9 dynamic-slice_add_fusion
  203.6 88.2 %all-gather.11.cloned.1.call-done = f32[1024,2176]{1,0:T(8,128)} async-done(((f32[256,2176]{1,0:T(8,128)}), f32[1024,2176]{1,0:T(8,128)}) %all-gather.11.cloned.1.call-update) | async-done | bytes 8912912 | tf_op jit(solution)/shard_map/all_gather | solution.py:40
  291.8 5.1 %select_reduce_fusion = (f32[256,2176]{1,0:T(8,128)S(1)}, f32[256,2176]{1,0:T(8,128)S(1)}) fusion(f32[4,256,2176]{2,1,0:T(8,128)} %bitcast.18, pred[4]{0:T(512)(128)(4,1)S(1)} %iota_compare_fusion.13), kind=kLoop, calls=%fused_computation | loop fusion | flops 5570560 | bytes 13369348 | tf_op jit(solution)/shard_map/reduce_sum | solution.py:15
  296.9 0.8 constant_dynamic-slice_fusion
  297.9 32.8 %all-gather.13.cloned.1.call-done = f32[256,2176]{1,0:T(8,128)} async-done(((f32[64,2176]{1,0:T(8,128)}), f32[256,2176]{1,0:T(8,128)}) %all-gather.13.cloned.1.call-update) | async-done | bytes 2228240 | tf_op jit(solution)/shard_map/all_gather | solution.py:45
  330.6 2.7 select_reduce_fusion.1
  333.4 32.3 %all-gather.9.cloned.1.call-done = f32[256,2176]{1,0:T(8,128)} async-done(((f32[64,2176]{1,0:T(8,128)}), f32[256,2176]{1,0:T(8,128)}) %all-gather.9.cloned.1.call-update) | async-done | bytes 2228240 | tf_op jit(solution)/shard_map/all_gather | solution.py:46
  365.7 3.2 add.97
  368.9 0.8 collective-permute-start.1
  369.7 4.1 collective-permute-done.1
  373.9 1.9 broadcast_select_fusion.1
  375.8 2.7 maximum_add_fusion
  378.5 0.5 slice.27
  379.1 2.5 collective-permute-start.2
  381.6 0.5 collective-permute-start.3
  382.2 0.6 collective-permute-start.4
  382.8 1.0 fusion
  383.8 8.2 %collective-permute-done.2 = f32[512,128]{1,0:T(8,128)S(1)} collective-permute-done((f32[512,128]{1,0:T(8,128)S(1)}, f32[512,128]{1,0:T(8,128)S(1)}, u32[]{:S(2)}, u32[]{:S(2)}) %collective-permute-start.2) | collective-permute-done | bytes 262176 | tf_op jit(solution)/shard_map/ppermute | solution.py:21
  392.0 3.9 collective-permute-done.4
  395.9 0.1 maximum_multiply_fusion
  395.9 1.8 fusion.13
  397.7 0.2 collective-permute-start.5
  397.9 0.5 collective-permute-start.6
  398.5 0.8 collective-permute-start.7
  399.3 6.0 %collective-permute-done.5 = f32[512,128]{1,0:T(8,128)S(1)} collective-permute-done((f32[512,128]{1,0:T(8,128)S(1)}, f32[512,128]{1,0:T(8,128)S(1)}, u32[]{:S(2)}, u32[]{:S(2)}) %collective-permute-start.5) | collective-permute-done | bytes 262176 | tf_op jit(solution)/shard_map/ppermute | solution.py:21
  405.3 1.7 collective-permute-done.6
  407.0 6.3 %collective-permute-done.7 = f32[512,128]{1,0:T(8,128)S(1)} collective-permute-done((f32[512,128]{1,0:T(8,128)S(1)}, f32[512,128]{1,0:T(8,128)S(1)}, u32[]{:S(2)}, u32[]{:S(2)}) %collective-permute-start.7) | collective-permute-done | bytes 262176 | tf_op jit(solution)/shard_map/ppermute | solution.py:21
  413.3 0.3 multiply_reduce_fusion.3
  413.6 0.3 multiply_reduce_fusion.2
  414.0 0.2 multiply_add_fusion.1
  414.2 1.8 fusion.12
  416.0 0.1 collective-permute-start.10
  416.1 2.7 collective-permute-start.8
  418.7 11.5 %collective-permute-done.10 = f32[512,128]{1,0:T(8,128)S(1)} collective-permute-done((f32[512,128]{1,0:T(8,128)S(1)}, f32[512,128]{1,0:T(8,128)S(1)}, u32[]{:S(2)}, u32[]{:S(2)}) %collective-permute-start.10) | collective-permute-done | bytes 262176 | tf_op jit(solution)/shard_map/ppermute | solution.py:21
  430.3 0.3 multiply_reduce_fusion.1
  430.6 0.4 copy-done.7
  431.0 0.1 copy-done.8
  431.1 0.1 copy-done.9
  431.2 1.9 multiply_reduce_fusion
  433.0 0.1 multiply_add_fusion
  433.1 0.7 copy-done.1
  433.9 1.9 fusion.18
  435.8 2.4 collective-permute-start.11
  438.1 0.7 collective-permute-start.13
  438.9 3.2 collective-permute-done.12
  442.1 0.3 add_convert_fusion
  442.4 2.2 fusion.14
  444.6 0.7 reshape.67
  445.3 8.7 %all-to-all-start.1 = ((bf16[32,20,128]{2,1,0:T(8,128)(2,1)}), bf16[32,20,128]{2,1,0:T(8,128)(2,1)S(1)}, u32[]{:S(2)}, u32[]{:S(2)}) async-start(bf16[32,20,128]{2,1,0:T(8,128)(2,1)} %reshape.67), calls=%async_computation.1 | async-start | bytes 393216 | tf_op jit(solution)/shard_map/all_to_all | solution.py:118
  454.0 0.2 copy.9
  454.1 8.1 %all-to-all-done.1 = bf16[32,20,128]{2,1,0:T(8,128)(2,1)S(1)} async-done(((bf16[32,20,128]{2,1,0:T(8,128)(2,1)}), bf16[32,20,128]{2,1,0:T(8,128)(2,1)S(1)}, u32[]{:S(2)}, u32[]{:S(2)}) %all-to-all-start.1) | async-done | bytes 163872 | tf_op jit(solution)/shard_map/all_to_all | solution.py:118
  462.3 0.5 multiply_reduce_fusion.5
  462.8 0.8 copy.10
  463.6 0.6 broadcast_multiply_fusion
  (42 shorter events, 0.4 us)
Async XLA Ops:
  7.2 171.6 %all-gather.7.cloned.1.call-start = ((), (), s32[]{:S(2)}) async-start(), calls=%async_computation.2 | async-start | bytes 13926400 | tf_op jit(solution)/shard_map/all_gather | solution.py:77
  74.9 216.8 %all-gather.11.cloned.1.call-start = ((), (), s32[]{:S(2)}) async-start(), calls=%async_computation.4 | async-start | bytes 11141120 | tf_op jit(solution)/shard_map/all_gather | solution.py:40
  191.2 8.3 %collective-permute-start = (f32[512,2176]{1,0:T(8,128)}, f32[512,2176]{1,0:T(8,128)}, u32[]{:S(2)}, u32[]{:S(2)}) collective-permute-start(f32[512,2176]{1,0:T(8,128)} %fusion.6), channel_id=1, source_target_pairs={{0,4},{4,0},{1,5},{5,1},{2,6},{6,2},{3,7},{7,3},{8,12},{12,8},{9,1... | collective-permute-start | bytes 13369352 | tf_op jit(solution)/shard_map/ppermute | solution.py:36
  203.5 127.1 %all-gather.13.cloned.1.call-start = ((), (), s32[]{:S(2)}) async-start(), calls=%async_computation.5 | async-start | bytes 2785280 | tf_op jit(solution)/shard_map/all_gather | solution.py:45
  297.8 67.9 %all-gather.9.cloned.1.call-start = ((), (), s32[]{:S(2)}) async-start(), calls=%async_computation.3 | async-start | bytes 2785280 | tf_op jit(solution)/shard_map/all_gather | solution.py:46
  368.9 5.0 %collective-permute-start.1 = (f32[256,2176]{1,0:T(8,128)}, f32[256,2176]{1,0:T(8,128)S(1)}, u32[]{:S(2)}, u32[]{:S(2)}) collective-permute-start(f32[256,2176]{1,0:T(8,128)} %add.97), channel_id=1, source_target_pairs={{0,4},{4,0},{1,5},{5,1},{2,6},{6,2},{3,7},{7,3},{8,12},{12,8},{9,1... | collective-permute-start | bytes 6684680 | tf_op jit(solution)/shard_map/ppermute | solution.py:48
  379.1 12.9 %collective-permute-start.2 = (f32[512,128]{1,0:T(8,128)S(1)}, f32[512,128]{1,0:T(8,128)S(1)}, u32[]{:S(2)}, u32[]{:S(2)}) collective-permute-start(f32[512,128]{1,0:T(8,128)S(1)} %slice.26), channel_id=1, source_target_pairs={{0,3},{1,0},{2,1},{3,2},{4,7},{5,4},{6,5},{7,6},{8,11},{9,8},{10,9... | collective-permute-start | bytes 786440 | tf_op jit(solution)/shard_map/ppermute | solution.py:21
  381.6 10.3 %collective-permute-start.3 = (f32[512,128]{1,0:T(8,128)S(1)}, f32[512,128]{1,0:T(8,128)S(1)}, u32[]{:S(2)}, u32[]{:S(2)}) collective-permute-start(f32[512,128]{1,0:T(8,128)S(1)} %slice.26), channel_id=1, source_target_pairs={{0,2},{1,3},{2,0},{3,1},{4,6},{5,7},{6,4},{7,5},{8,10},{9,11},{10,... | collective-permute-start | bytes 786440 | tf_op jit(solution)/shard_map/ppermute | solution.py:21
  382.2 13.7 %collective-permute-start.4 = (f32[512,128]{1,0:T(8,128)S(1)}, f32[512,128]{1,0:T(8,128)S(1)}, u32[]{:S(2)}, u32[]{:S(2)}) collective-permute-start(f32[512,128]{1,0:T(8,128)S(1)} %slice.26), channel_id=1, source_target_pairs={{0,1},{1,2},{2,3},{3,0},{4,5},{5,6},{6,7},{7,4},{8,9},{9,10},{10,1... | collective-permute-start | bytes 786440 | tf_op jit(solution)/shard_map/ppermute | solution.py:21
  383.8 30.4 %copy-start = (f32[512,2048]{1,0:T(8,128)}, f32[512,2048]{1,0:T(8,128)S(1)}, u32[]{:S(2)}) copy-start(f32[512,2048]{1,0:T(8,128)S(1)} %fusion) | copy-start | bytes 12582916
  397.7 7.5 %collective-permute-start.5 = (f32[512,128]{1,0:T(8,128)S(1)}, f32[512,128]{1,0:T(8,128)S(1)}, u32[]{:S(2)}, u32[]{:S(2)}) collective-permute-start(f32[512,128]{1,0:T(8,128)S(1)} %fusion.13), channel_id=1, source_target_pairs={{0,3},{1,0},{2,1},{3,2},{4,7},{5,4},{6,5},{7,6},{8,11},{9,8},{10,9... | collective-permute-start | bytes 786440 | tf_op jit(solution)/shard_map/ppermute | solution.py:21
  397.9 9.0 %collective-permute-start.6 = (f32[512,128]{1,0:T(8,128)S(1)}, f32[512,128]{1,0:T(8,128)S(1)}, u32[]{:S(2)}, u32[]{:S(2)}) collective-permute-start(f32[512,128]{1,0:T(8,128)S(1)} %fusion.13), channel_id=1, source_target_pairs={{0,2},{1,3},{2,0},{3,1},{4,6},{5,7},{6,4},{7,5},{8,10},{9,11},{10,... | collective-permute-start | bytes 786440 | tf_op jit(solution)/shard_map/ppermute | solution.py:21
  398.5 14.8 %collective-permute-start.7 = (f32[512,128]{1,0:T(8,128)S(1)}, f32[512,128]{1,0:T(8,128)S(1)}, u32[]{:S(2)}, u32[]{:S(2)}) collective-permute-start(f32[512,128]{1,0:T(8,128)S(1)} %fusion.13), channel_id=1, source_target_pairs={{0,1},{1,2},{2,3},{3,0},{4,5},{5,6},{6,7},{7,4},{8,9},{9,10},{10,1... | collective-permute-start | bytes 786440 | tf_op jit(solution)/shard_map/ppermute | solution.py:21
  405.3 8.7 %copy-start.3 = (f32[512,128]{1,0:T(8,128)}, f32[512,128]{1,0:T(8,128)S(1)}, u32[]{:S(2)}) copy-start(f32[512,128]{1,0:T(8,128)S(1)} %collective-permute-done.5) | copy-start | bytes 786436
  407.0 7.0 %copy-start.4 = (f32[512,128]{1,0:T(8,128)}, f32[512,128]{1,0:T(8,128)S(1)}, u32[]{:S(2)}) copy-start(f32[512,128]{1,0:T(8,128)S(1)} %collective-permute-done.6) | copy-start | bytes 786436
  413.3 0.7 copy-start.5
  416.0 14.6 %copy-start.6 = (f32[512,128]{1,0:T(8,128)}, f32[512,128]{1,0:T(8,128)S(1)}, u32[]{:S(2)}) copy-start(f32[512,128]{1,0:T(8,128)S(1)} %fusion.12) | copy-start | bytes 786436
  416.0 14.3 %collective-permute-start.10 = (f32[512,128]{1,0:T(8,128)S(1)}, f32[512,128]{1,0:T(8,128)S(1)}, u32[]{:S(2)}, u32[]{:S(2)}) collective-permute-start(f32[512,128]{1,0:T(8,128)S(1)} %fusion.12), channel_id=1, source_target_pairs={{0,1},{1,2},{2,3},{3,0},{4,5},{5,6},{6,7},{7,4},{8,9},{9,10},{10,1... | collective-permute-start | bytes 786440 | tf_op jit(solution)/shard_map/ppermute | solution.py:21
  416.1 14.2 %collective-permute-start.8 = (f32[512,128]{1,0:T(8,128)S(1)}, f32[512,128]{1,0:T(8,128)S(1)}, u32[]{:S(2)}, u32[]{:S(2)}) collective-permute-start(f32[512,128]{1,0:T(8,128)S(1)} %fusion.12), channel_id=1, source_target_pairs={{0,3},{1,0},{2,1},{3,2},{4,7},{5,4},{6,5},{7,6},{8,11},{9,8},{10,9... | collective-permute-start | bytes 786440 | tf_op jit(solution)/shard_map/ppermute | solution.py:21
  418.7 11.5 %collective-permute-start.9 = (f32[512,128]{1,0:T(8,128)S(1)}, f32[512,128]{1,0:T(8,128)S(1)}, u32[]{:S(2)}, u32[]{:S(2)}) collective-permute-start(f32[512,128]{1,0:T(8,128)S(1)} %fusion.12), channel_id=1, source_target_pairs={{0,2},{1,3},{2,0},{3,1},{4,6},{5,7},{6,4},{7,5},{8,10},{9,11},{10,... | collective-permute-start | bytes 786440 | tf_op jit(solution)/shard_map/ppermute | solution.py:21
  430.3 0.7 copy-start.7
  430.3 0.8 copy-start.8
  430.3 0.9 copy-start.9
  431.1 2.7 copy-start.1
  435.8 3.1 collective-permute-start.11
  438.1 3.9 collective-permute-start.12
  438.1 3.9 collective-permute-start.13
  438.8 3.6 copy-start.2
  442.4 11.6 %copy-start.10 = (bf16[640,128]{1,0:T(8,128)(2,1)S(1)}, bf16[640,128]{1,0:T(8,128)(2,1)}, u32[]{:S(2)}) copy-start(bf16[640,128]{1,0:T(8,128)(2,1)} %param.4) | copy-start | bytes 491524
  445.3 17.0 %all-to-all-start.1 = ((bf16[32,20,128]{2,1,0:T(8,128)(2,1)}), bf16[32,20,128]{2,1,0:T(8,128)(2,1)S(1)}, u32[]{:S(2)}, u32[]{:S(2)}) async-start(bf16[32,20,128]{2,1,0:T(8,128)(2,1)} %reshape.67), calls=%async_computation.1 | async-start | bytes 393216 | tf_op jit(solution)/shard_map/all_to_all | solution.py:118
Sparse Core Ops, SparseCore 0:
  75.1 103.6 all-gather.6
  203.6 88.1 all-gather.10
  297.9 32.6 all-gather.12
  333.5 32.1 all-gather.8
where the time goes:
time: 471 us
  waiting for transfers between devices  318 us (68%)
  blocking collectives  51.3 us (11%)
  matrix products  27.4 us (6%)
  other arithmetic  25.3 us (5%)
  starting transfers between devices  21.5 us (5%)
  between operations  14 us (3%)
  local copies, waits for them, and re-layouts  13.3 us (3%)
    all_gather x1, waiting for transfers between devices, body(): rows_xy = lax.all_gather(local_xy, 'feat', axis=0, tiled=True)  104 us
    all_gather x1, waiting for transfers between devices, exclusive_prefix(): along_z = lax.all_gather(mine, 'z')  88.2 us
    all_to_all x1, blocking collectives, body(): lax.all_to_all(sorted_xy, TM, split_axis=0, concat_axis=0, tiled=True)  51.3 us
    ppermute x12, waiting for transfers between devices, gather_feat(): lax.ppermute(piece, 'feat', [(i, (i - k) % n) for i in range(n)])  40.9 us
    all_gather x1, waiting for transfers between devices, exclusive_prefix(): along_x = lax.all_gather(piece, 'x')  32.8 us
    all_gather x1, waiting for transfers between devices, exclusive_prefix(): before_x = lax.all_gather(masked_sum(along_x, xi), 'z', axis=0, tiled=True)  32.3 us
    dot_general x1, matrix products, body(): lax.dot_general(own, rows_xy, contract, preferred_element_type=jnp.float32)  12.5 us
    ppermute x12, starting transfers between devices, gather_feat(): lax.ppermute(piece, 'feat', [(i, (i - k) % n) for i in range(n)])  11 us
  transfers between devices with their start and end apart: 19, of which 14 were waited for; matrix products, arithmetic and copies ran while one was open for 0% of the time, Pallas kernels for 0%

commit v1 on v0

--- a/solution.py
+++ b/solution.py
@@ -8,6 +8,24 @@
 TINY = 1e-06
 TM = ("x", "z", "c")
 SWAP = [(0, 1), (1, 0)]
+
+
+def gather_around(shard, axis, dim):
+    ways, here, step = (lax.axis_size(axis), lax.axis_index(axis), shard.shape[dim])
+    lengths = [n * ways if d == dim else n for d, n in enumerate(shard.shape)]
+    full = lax.dynamic_update_slice_in_dim(
+        jnp.zeros(lengths, shard.dtype), shard, here * step, axis=dim
+    )
+    going_up = going_down = shard
+    for far in range(1, ways // 2 + 1):
+        going_up = lax.ppermute(going_up, axis, [(d, (d + 1) % ways) for d in range(ways)])
+        full = lax.dynamic_update_slice_in_dim(full, going_up, (here - far) % ways * step, axis=dim)
+        if 2 * far < ways:
+            going_down = lax.ppermute(going_down, axis, [(d, (d - 1) % ways) for d in range(ways)])
+            full = lax.dynamic_update_slice_in_dim(
+                full, going_down, (here + far) % ways * step, axis=dim
+            )
+    return full
 
 
 def masked_sum(stack, position):
@@ -74,7 +92,7 @@
     local_xy = moved.reshape(tok_dev, width + n_targets)
     local_x = local_xy[:, :width]
     col_start = lax.axis_index("feat") * block_rows
-    rows_xy = lax.all_gather(local_xy, "feat", axis=0, tiled=True)
+    rows_xy = gather_around(local_xy, "feat", 0)
     own = lax.dynamic_slice_in_dim(rows_xy, col_start, block_rows, 1)
     moments = exclusive_prefix(
         lax.dot_general(own, rows_xy, contract, preferred_element_type=jnp.float32)

time: 471 us -> 488 us (1.036)
  local copies, waits for them, and re-layouts: 13.3 us -> 22.9 us
  waiting for transfers between devices: 318 us -> 324 us
    ppermute x0 -> x3, waiting for transfers between devices: none -> 116 us  [the longest x2 116 us: gather_around(): lax.ppermute(going_up, axis, [(d, (d + 1) % ways) for d in range(ways)])]
    all_gather x1 -> x0, waiting for transfers between devices: 104 us -> none  [body(): rows_xy = lax.all_gather(local_xy, 'feat', axis=0, tiled=True)]
    dynamic_update_slice x0 -> x4, local copies, waits for them, and re-layouts: none -> 8.73 us  [the longest x2 4.36 us: gather_around(): lax.dynamic_update_slice_in_dim(full, going_up, (here - far) % ways * ste...]
    all_gather x1, waiting for transfers between devices: 88.2 us -> 82.3 us  [exclusive_prefix(): along_z = lax.all_gather(mine, 'z')]
  transfers between devices with their start and end apart: 19 -> 21, of which waited for: 14 -> 17; matrix products, arithmetic and copies ran while one was open for 0% -> 2% of each run, Pallas kernels for 0% -> 0%
where the time goes in v1:
time: 488 us; the launch traced here: 487 us
  waiting for transfers between devices  324 us (66%)
  blocking collectives  51.3 us (11%)
  other arithmetic  25.3 us (5%)
  matrix products  24.7 us (5%)
  starting transfers between devices  24.6 us (5%)
  local copies, waits for them, and re-layouts  22.9 us (5%)
  between operations  14 us (3%)
    ppermute x2, waiting for transfers between devices, gather_around(): lax.ppermute(going_up, axis, [(d, (d + 1) % ways) for d in range(ways)])  116 us
    all_gather x1, waiting for transfers between devices, exclusive_prefix(): along_z = lax.all_gather(mine, 'z')  82.3 us
    all_to_all x1, blocking collectives, body(): lax.all_to_all(sorted_xy, TM, split_axis=0, concat_axis=0, tiled=True)  51.3 us
    ppermute x12, waiting for transfers between devices, gather_feat(): lax.ppermute(piece, 'feat', [(i, (i - k) % n) for i in range(n)])  41.1 us
    all_gather x1, waiting for transfers between devices, exclusive_prefix(): along_x = lax.all_gather(piece, 'x')  32.8 us
    all_gather x1, waiting for transfers between devices, exclusive_prefix(): before_x = lax.all_gather(masked_sum(along_x, xi), 'z', axis=0, tiled=True)  32.3 us
    ppermute x12, starting transfers between devices, gather_feat(): lax.ppermute(piece, 'feat', [(i, (i - k) % n) for i in range(n)])  11 us
  transfers between devices with their start and end apart: 21, of which 17 were waited for; matrix products, arithmetic and copies ran while one was open for 2% of the time, Pallas kernels for 0%

profile of v1, /device:TPU:1, one launch (start us, length us, event | category | flops | bytes accessed | tf_op | source)
XLA Modules:
  0.0 486.7 jit_solution(2303873230479915043)
XLA Ops:
  7.2 1.1 fusion.20
  8.3 0.7 convert_add_fusion
  9.0 5.8 %convolution_convert_fusion = bf16[640,2176]{1,0:T(8,128)(2,1)} fusion(bf16[640,128]{1,0:T(8,128)(2,1)} %param.4, bf16[640,2048]{1,0:T(8,128)(2,1)} %param.3, s32[640]{0:T(1024)S(1)} %convert_add_fusion), kind=kOutput, calls=%fused_computation.3 | convolution fusion | flops 1789952000 | bytes 5573120 | tf_op jit(solution)/shard_map/dot_general | solution.py:89
  14.7 3.6 reshape.65
  18.3 51.3 %all_to_all.10 = bf16[32,20,2176]{2,1,0:T(8,128)(2,1)} all-to-all(bf16[32,20,2176]{2,1,0:T(8,128)(2,1)S(1)} %reshape.65), channel_id=1, replica_groups=mesh['x'=4,'z'=4,'c'=2,'feat'=4] {'x','z','c'}, dimensions={0} | all-to-all | bytes 5570560 | tf_op jit(solution)/shard_map/all_to_all | solution.py:91
  69.7 5.3 %reshape.66 = bf16[640,2176]{1,0:T(8,128)(2,1)} reshape(bf16[32,20,2176]{2,1,0:T(8,128)(2,1)} %all_to_all.10) | data formatting | bytes 5570560 | tf_op jit(solution)/shard_map/reshape | solution.py:92
  74.9 1.3 collective-permute-start
  76.2 1.4 collective-permute-start.1
  77.7 60.5 %collective-permute-done = bf16[640,2176]{1,0:T(8,128)(2,1)} collective-permute-done((bf16[640,2176]{1,0:T(8,128)(2,1)}, bf16[640,2176]{1,0:T(8,128)(2,1)}, u32[]{:S(2)}, u32[]{:S(2)}) %collective-permute-start) | collective-permute-done | bytes 2785312 | tf_op jit(solution)/shard_map/ppermute | solution.py:21
  138.2 0.8 broadcast_in_dim.48
  139.0 2.2 constant_dynamic-update-slice_fusion.3
  141.2 2.2 constant_dynamic-update-slice_fusion.2
  143.4 2.2 constant_dynamic-update-slice_fusion.1
  145.6 55.0 %collective-permute-done.2 = bf16[640,2176]{1,0:T(8,128)(2,1)} collective-permute-done((bf16[640,2176]{1,0:T(8,128)(2,1)}, bf16[640,2176]{1,0:T(8,128)(2,1)}, u32[]{:S(2)}, u32[]{:S(2)}) %collective-permute-start.2) | collective-permute-done | bytes 2785312 | tf_op jit(solution)/shard_map/ppermute | solution.py:21
  200.6 2.2 constant_dynamic-update-slice_fusion
  202.8 8.0 %fusion.6 = f32[512,2176]{1,0:T(8,128)} fusion(bf16[2560,2176]{1,0:T(8,128)(2,1)S(1)} %constant_dynamic-update-slice_fusion, s32[]{:T(128)S(6)} %select_n.82), kind=kOutput, calls=%fused_computation.11 | convolution fusion | flops 5704253440 | bytes 18219012 | tf_op jit(solution)/shard_map/dot_general | solution.py:98
  210.7 2.0 collective-permute-start.3
  212.7 7.5 %collective-permute-done.3 = f32[512,2176]{1,0:T(8,128)} collective-permute-done((f32[512,2176]{1,0:T(8,128)}, f32[512,2176]{1,0:T(8,128)}, u32[]{:S(2)}, u32[]{:S(2)}) %collective-permute-start.3) | collective-permute-done | bytes 4456480 | tf_op jit(solution)/shard_map/ppermute | solution.py:54
  220.2 3.9 dynamic-slice_add_fusion
  224.4 82.3 %all-gather.8.cloned.1.call-done = f32[1024,2176]{1,0:T(8,128)} async-done(((f32[256,2176]{1,0:T(8,128)}), f32[1024,2176]{1,0:T(8,128)}) %all-gather.8.cloned.1.call-update) | async-done | bytes 8912912 | tf_op jit(solution)/shard_map/all_gather | solution.py:58
  306.6 5.1 %select_reduce_fusion = (f32[256,2176]{1,0:T(8,128)S(1)}, f32[256,2176]{1,0:T(8,128)S(1)}) fusion(f32[4,256,2176]{2,1,0:T(8,128)} %bitcast.18, pred[4]{0:T(512)(128)(4,1)S(1)} %iota_compare_fusion.13), kind=kLoop, calls=%fused_computation | loop fusion | flops 5570560 | bytes 13369348 | tf_op jit(solution)/shard_map/reduce_sum | solution.py:33
  311.7 0.8 constant_dynamic-slice_fusion
  312.7 32.8 %all-gather.10.cloned.1.call-done = f32[256,2176]{1,0:T(8,128)} async-done(((f32[64,2176]{1,0:T(8,128)}), f32[256,2176]{1,0:T(8,128)}) %all-gather.10.cloned.1.call-update) | async-done | bytes 2228240 | tf_op jit(solution)/shard_map/all_gather | solution.py:63
  345.5 2.7 select_reduce_fusion.1
  348.2 32.3 %all-gather.6.cloned.1.call-done = f32[256,2176]{1,0:T(8,128)} async-done(((f32[64,2176]{1,0:T(8,128)}), f32[256,2176]{1,0:T(8,128)}) %all-gather.6.cloned.1.call-update) | async-done | bytes 2228240 | tf_op jit(solution)/shard_map/all_gather | solution.py:64
  380.5 3.2 add.131
  383.7 0.8 collective-permute-start.4
  384.6 4.1 collective-permute-done.4
  388.7 1.9 broadcast_select_fusion.1
  390.6 2.7 maximum_add_fusion
  393.4 0.5 slice.27
  393.9 2.5 collective-permute-start.5
  396.5 0.5 collective-permute-start.6
  397.0 0.6 collective-permute-start.7
  397.6 1.0 fusion
  398.6 8.2 %collective-permute-done.5 = f32[512,128]{1,0:T(8,128)S(1)} collective-permute-done((f32[512,128]{1,0:T(8,128)S(1)}, f32[512,128]{1,0:T(8,128)S(1)}, u32[]{:S(2)}, u32[]{:S(2)}) %collective-permute-start.5) | collective-permute-done | bytes 262176 | tf_op jit(solution)/shard_map/ppermute | solution.py:39
  406.8 3.9 collective-permute-done.7
  410.8 1.8 fusion.13
  412.7 2.7 collective-permute-start.8
  415.3 11.6 %collective-permute-done.10 = f32[512,128]{1,0:T(8,128)S(1)} collective-permute-done((f32[512,128]{1,0:T(8,128)S(1)}, f32[512,128]{1,0:T(8,128)S(1)}, u32[]{:S(2)}, u32[]{:S(2)}) %collective-permute-start.10) | collective-permute-done | bytes 262176 | tf_op jit(solution)/shard_map/ppermute | solution.py:39
  427.0 0.3 multiply_reduce_fusion.3
  427.3 0.3 multiply_reduce_fusion.2
  428.1 1.8 fusion.12
  429.9 2.4 collective-permute-start.11
  432.2 0.7 collective-permute-start.13
  432.9 3.8 collective-permute-done.11
  436.7 3.2 collective-permute-done.12
  439.9 7.1 %collective-permute-done.13 = f32[512,128]{1,0:T(8,128)S(1)} collective-permute-done((f32[512,128]{1,0:T(8,128)S(1)}, f32[512,128]{1,0:T(8,128)S(1)}, u32[]{:S(2)}, u32[]{:S(2)}) %collective-permute-start.13) | collective-permute-done | bytes 262176 | tf_op jit(solution)/shard_map/ppermute | solution.py:39
  447.3 0.4 copy-done.8
  447.7 1.9 multiply_reduce_fusion
  449.7 0.7 copy-done.1
  450.5 1.9 fusion.18
  452.4 0.5 collective-permute-start.15
  452.9 0.9 collective-permute-start.16
  453.9 0.9 collective-permute-done.14
  454.8 1.6 collective-permute-done.15
  456.4 0.8 collective-permute-done.16
  457.5 3.9 fusion.14
  461.4 0.7 reshape.67
  462.1 7.8 %all-to-all-start.1 = ((bf16[32,20,128]{2,1,0:T(8,128)(2,1)}), bf16[32,20,128]{2,1,0:T(8,128)(2,1)S(1)}, u32[]{:S(2)}, u32[]{:S(2)}) async-start(bf16[32,20,128]{2,1,0:T(8,128)(2,1)} %reshape.67), calls=%async_computation.1 | async-start | bytes 393216 | tf_op jit(solution)/shard_map/all_to_all | solution.py:136
  470.1 8.1 %all-to-all-done.1 = bf16[32,20,128]{2,1,0:T(8,128)(2,1)S(1)} async-done(((bf16[32,20,128]{2,1,0:T(8,128)(2,1)}), bf16[32,20,128]{2,1,0:T(8,128)(2,1)S(1)}, u32[]{:S(2)}, u32[]{:S(2)}) %all-to-all-start.1) | async-done | bytes 163872 | tf_op jit(solution)/shard_map/all_to_all | solution.py:136
  478.3 0.5 multiply_reduce_fusion.5
  478.8 0.8 copy.10
  479.6 0.6 broadcast_multiply_fusion
  (48 shorter events, 2.0 us)
Async XLA Ops:
  7.2 299.5 %all-gather.8.cloned.1.call-start = ((), (), s32[]{:S(2)}) async-start(), calls=%async_computation.3 | async-start | bytes 11141120 | tf_op jit(solution)/shard_map/all_gather | solution.py:58
  74.9 63.3 %collective-permute-start = (bf16[640,2176]{1,0:T(8,128)(2,1)}, bf16[640,2176]{1,0:T(8,128)(2,1)}, u32[]{:S(2)}, u32[]{:S(2)}) collective-permute-start(bf16[640,2176]{1,0:T(8,128)(2,1)} %reshape.66), channel_id=1, source_target_pairs={{0,1},{1,2},{2,3},{3,0},{4,5},{5,6},{6,7},{7,4},{8,9},{9,10},{10,1... | collective-permute-start | bytes 8355848 | tf_op jit(solution)/shard_map/ppermute | solution.py:21
  76.2 67.1 %collective-permute-start.1 = (bf16[640,2176]{1,0:T(8,128)(2,1)}, bf16[640,2176]{1,0:T(8,128)(2,1)}, u32[]{:S(2)}, u32[]{:S(2)}) collective-permute-start(bf16[640,2176]{1,0:T(8,128)(2,1)} %reshape.66), channel_id=1, source_target_pairs={{0,3},{1,0},{2,1},{3,2},{4,7},{5,4},{6,5},{7,6},{8,11},{9,8},{10,9... | collective-permute-start | bytes 8355848 | tf_op jit(solution)/shard_map/ppermute | solution.py:24
  138.2 62.4 %collective-permute-start.2 = (bf16[640,2176]{1,0:T(8,128)(2,1)}, bf16[640,2176]{1,0:T(8,128)(2,1)}, u32[]{:S(2)}, u32[]{:S(2)}) collective-permute-start(bf16[640,2176]{1,0:T(8,128)(2,1)} %collective-permute-done), channel_id=1, source_target_pairs={{0,1},{1,2},{2,3},{3,0},{4,5},{5,6},{6,7},{7,4},{8,9},{9,10},{10,1... | collective-permute-start | bytes 8355848 | tf_op jit(solution)/shard_map/ppermute | solution.py:21
  210.7 9.5 %collective-permute-start.3 = (f32[512,2176]{1,0:T(8,128)}, f32[512,2176]{1,0:T(8,128)}, u32[]{:S(2)}, u32[]{:S(2)}) collective-permute-start(f32[512,2176]{1,0:T(8,128)} %fusion.6), channel_id=1, source_target_pairs={{0,4},{4,0},{1,5},{5,1},{2,6},{6,2},{3,7},{7,3},{8,12},{12,8},{9,1... | collective-permute-start | bytes 13369352 | tf_op jit(solution)/shard_map/ppermute | solution.py:54
  224.1 121.4 %all-gather.10.cloned.1.call-start = ((), (), s32[]{:S(2)}) async-start(), calls=%async_computation.4 | async-start | bytes 2785280 | tf_op jit(solution)/shard_map/all_gather | solution.py:63
  312.6 67.9 %all-gather.6.cloned.1.call-start = ((), (), s32[]{:S(2)}) async-start(), calls=%async_computation.2 | async-start | bytes 2785280 | tf_op jit(solution)/shard_map/all_gather | solution.py:64
  383.7 5.0 %collective-permute-start.4 = (f32[256,2176]{1,0:T(8,128)}, f32[256,2176]{1,0:T(8,128)S(1)}, u32[]{:S(2)}, u32[]{:S(2)}) collective-permute-start(f32[256,2176]{1,0:T(8,128)} %add.131), channel_id=1, source_target_pairs={{0,4},{4,0},{1,5},{5,1},{2,6},{6,2},{3,7},{7,3},{8,12},{12,8},{9,1... | collective-permute-start | bytes 6684680 | tf_op jit(solution)/shard_map/ppermute | solution.py:66
  393.9 12.9 %collective-permute-start.5 = (f32[512,128]{1,0:T(8,128)S(1)}, f32[512,128]{1,0:T(8,128)S(1)}, u32[]{:S(2)}, u32[]{:S(2)}) collective-permute-start(f32[512,128]{1,0:T(8,128)S(1)} %slice.26), channel_id=1, source_target_pairs={{0,3},{1,0},{2,1},{3,2},{4,7},{5,4},{6,5},{7,6},{8,11},{9,8},{10,9... | collective-permute-start | bytes 786440 | tf_op jit(solution)/shard_map/ppermute | solution.py:39
  396.5 10.3 %collective-permute-start.6 = (f32[512,128]{1,0:T(8,128)S(1)}, f32[512,128]{1,0:T(8,128)S(1)}, u32[]{:S(2)}, u32[]{:S(2)}) collective-permute-start(f32[512,128]{1,0:T(8,128)S(1)} %slice.26), channel_id=1, source_target_pairs={{0,2},{1,3},{2,0},{3,1},{4,6},{5,7},{6,4},{7,5},{8,10},{9,11},{10,... | collective-permute-start | bytes 786440 | tf_op jit(solution)/shard_map/ppermute | solution.py:39
  397.0 13.7 %collective-permute-start.7 = (f32[512,128]{1,0:T(8,128)S(1)}, f32[512,128]{1,0:T(8,128)S(1)}, u32[]{:S(2)}, u32[]{:S(2)}) collective-permute-start(f32[512,128]{1,0:T(8,128)S(1)} %slice.26), channel_id=1, source_target_pairs={{0,1},{1,2},{2,3},{3,0},{4,5},{5,6},{6,7},{7,4},{8,9},{9,10},{10,1... | collective-permute-start | bytes 786440 | tf_op jit(solution)/shard_map/ppermute | solution.py:39
  398.6 29.4 %copy-start = (f32[512,2048]{1,0:T(8,128)}, f32[512,2048]{1,0:T(8,128)S(1)}, u32[]{:S(2)}) copy-start(f32[512,2048]{1,0:T(8,128)S(1)} %fusion) | copy-start | bytes 12582916
  412.6 14.4 %collective-permute-start.10 = (f32[512,128]{1,0:T(8,128)S(1)}, f32[512,128]{1,0:T(8,128)S(1)}, u32[]{:S(2)}, u32[]{:S(2)}) collective-permute-start(f32[512,128]{1,0:T(8,128)S(1)} %fusion.13), channel_id=1, source_target_pairs={{0,1},{1,2},{2,3},{3,0},{4,5},{5,6},{6,7},{7,4},{8,9},{9,10},{10,1... | collective-permute-start | bytes 786440 | tf_op jit(solution)/shard_map/ppermute | solution.py:39
  412.7 14.3 %collective-permute-start.8 = (f32[512,128]{1,0:T(8,128)S(1)}, f32[512,128]{1,0:T(8,128)S(1)}, u32[]{:S(2)}, u32[]{:S(2)}) collective-permute-start(f32[512,128]{1,0:T(8,128)S(1)} %fusion.13), channel_id=1, source_target_pairs={{0,3},{1,0},{2,1},{3,2},{4,7},{5,4},{6,5},{7,6},{8,11},{9,8},{10,9... | collective-permute-start | bytes 786440 | tf_op jit(solution)/shard_map/ppermute | solution.py:39
  415.3 11.6 %collective-permute-start.9 = (f32[512,128]{1,0:T(8,128)S(1)}, f32[512,128]{1,0:T(8,128)S(1)}, u32[]{:S(2)}, u32[]{:S(2)}) collective-permute-start(f32[512,128]{1,0:T(8,128)S(1)} %fusion.13), channel_id=1, source_target_pairs={{0,2},{1,3},{2,0},{3,1},{4,6},{5,7},{6,4},{7,5},{8,10},{9,11},{10,... | collective-permute-start | bytes 786440 | tf_op jit(solution)/shard_map/ppermute | solution.py:39
  426.9 0.7 copy-start.2
  427.0 0.8 copy-start.3
  427.0 0.9 copy-start.4
  429.9 17.4 %copy-start.5 = (f32[512,128]{1,0:T(8,128)}, f32[512,128]{1,0:T(8,128)S(1)}, u32[]{:S(2)}) copy-start(f32[512,128]{1,0:T(8,128)S(1)} %fusion.12) | copy-start | bytes 786436
  429.9 6.8 %collective-permute-start.11 = (f32[512,128]{1,0:T(8,128)S(1)}, f32[512,128]{1,0:T(8,128)S(1)}, u32[]{:S(2)}, u32[]{:S(2)}) collective-permute-start(f32[512,128]{1,0:T(8,128)S(1)} %fusion.12), channel_id=1, source_target_pairs={{0,3},{1,0},{2,1},{3,2},{4,7},{5,4},{6,5},{7,6},{8,11},{9,8},{10,9... | collective-permute-start | bytes 786440 | tf_op jit(solution)/shard_map/ppermute | solution.py:39
  432.2 7.6 %collective-permute-start.12 = (f32[512,128]{1,0:T(8,128)S(1)}, f32[512,128]{1,0:T(8,128)S(1)}, u32[]{:S(2)}, u32[]{:S(2)}) collective-permute-start(f32[512,128]{1,0:T(8,128)S(1)} %fusion.12), channel_id=1, source_target_pairs={{0,2},{1,3},{2,0},{3,1},{4,6},{5,7},{6,4},{7,5},{8,10},{9,11},{10,... | collective-permute-start | bytes 786440 | tf_op jit(solution)/shard_map/ppermute | solution.py:39
  432.2 14.8 %collective-permute-start.13 = (f32[512,128]{1,0:T(8,128)S(1)}, f32[512,128]{1,0:T(8,128)S(1)}, u32[]{:S(2)}, u32[]{:S(2)}) collective-permute-start(f32[512,128]{1,0:T(8,128)S(1)} %fusion.12), channel_id=1, source_target_pairs={{0,1},{1,2},{2,3},{3,0},{4,5},{5,6},{6,7},{7,4},{8,9},{9,10},{10,1... | collective-permute-start | bytes 786440 | tf_op jit(solution)/shard_map/ppermute | solution.py:39
  436.7 10.6 %copy-start.6 = (f32[512,128]{1,0:T(8,128)}, f32[512,128]{1,0:T(8,128)S(1)}, u32[]{:S(2)}) copy-start(f32[512,128]{1,0:T(8,128)S(1)} %collective-permute-done.11) | copy-start | bytes 786436
  439.9 7.4 %copy-start.7 = (f32[512,128]{1,0:T(8,128)}, f32[512,128]{1,0:T(8,128)S(1)}, u32[]{:S(2)}) copy-start(f32[512,128]{1,0:T(8,128)S(1)} %collective-permute-done.12) | copy-start | bytes 786436
  447.0 0.7 copy-start.8
  447.7 2.7 copy-start.1
  452.3 2.5 collective-permute-start.14
  452.4 4.0 collective-permute-start.15
  452.9 4.3 collective-permute-start.16
  457.5 12.5 %copy-start.9 = (bf16[640,128]{1,0:T(8,128)(2,1)S(1)}, bf16[640,128]{1,0:T(8,128)(2,1)}, u32[]{:S(2)}) copy-start(bf16[640,128]{1,0:T(8,128)(2,1)} %param.4) | copy-start | bytes 491524
  462.1 16.1 %all-to-all-start.1 = ((bf16[32,20,128]{2,1,0:T(8,128)(2,1)}), bf16[32,20,128]{2,1,0:T(8,128)(2,1)S(1)}, u32[]{:S(2)}, u32[]{:S(2)}) async-start(bf16[32,20,128]{2,1,0:T(8,128)(2,1)} %reshape.67), calls=%async_computation.1 | async-start | bytes 393216 | tf_op jit(solution)/shard_map/all_to_all | solution.py:136
Sparse Core Ops, SparseCore 0:
  224.2 82.3 all-gather.7
  312.7 32.6 all-gather.9
  348.3 32.1 all-gather.5
